TPU v7x, 32 devices: a whole 2x2x4 slice. The times are simulated.
32 devices in a mesh: groups: 2 (over x), dp: 4 (over y, core), hidden: 4 (over z).
Axes of the slice: x: 2, y: 2, z: 4, core: 2. Of those that a mesh axis runs over, the one named last changes fastest.
Arguments:
- activations: bfloat16 [24576, 8192], P(('groups', 'dp'), 'hidden'), parts along dimension 0, may hold values from -6 to 6
- cotangent: bfloat16 [24576, 8192], P(('groups', 'dp'), 'hidden'), parts along dimension 0
- up_factor_matrix: bfloat16 [8192, 64], P('hidden'), may hold values from -0.0625 to 0.0625
- input_sketch: bfloat16 [8192, 128], P('hidden'), may hold values from -0.0625 to 0.0625
- rank_sketch: float32 [64, 32], replicated, may hold values from -0.75 to 0.75
Outputs:
- features: bfloat16 [48, 4096], P(('groups', 'dp'), 'hidden'), parts along dimension 0
- scores: float32 [48, 24], P(('groups', 'dp'), 'hidden'), parts along dimension 0
There are 2 independent parts, one for each index of `groups`. A program takes and returns all parts, laid end to end along the dimension named above; an argument that names none is the same for every part. Nothing has to cross between parts.
All inputs are finite; a program needn't handle non-finite values.
Results may differ from a plain program's by a relative error of at most 0.0017.
Values may be sent and summed in bfloat16 or wider, within the bound.
No kernel may reach another device: no remote copies, remote signals or barrier semaphores. Data moves between devices by JAX's collectives and lax.ppermute only.
A program may use at most 64 MiB of HBM per device.

v0:
```python
import math
import jax
import jax.numpy as jnp
from jax import lax
from jax.sharding import PartitionSpec as P

SEQ = 512
epsilon = 1e-05
HI = lax.Precision.HIGHEST


def partial_features(activations, cotangent, up_factor_matrix, input_sketch, rank_sketch):
    examples = activations.shape[0] // SEQ
    backward_pass = jnp.dot(cotangent, up_factor_matrix, preferred_element_type=jnp.float32)
    rank_part = jnp.dot(backward_pass, rank_sketch, precision=HI)
    rank_full = lax.psum(rank_part, "hidden")
    input_part = jnp.dot(activations, input_sketch, preferred_element_type=jnp.float32)
    rank_rows = rank_full.reshape(examples, SEQ, rank_full.shape[1])
    input_rows = input_part.reshape(examples, SEQ, input_part.shape[1])
    return jnp.einsum("esa,esb->eab", rank_rows, input_rows, precision=HI)


def per_device(activations, cotangent, up_factor_matrix, input_sketch, rank_sketch):
    examples = activations.shape[0] // SEQ
    partial = partial_features(activations, cotangent, up_factor_matrix, input_sketch, rank_sketch)
    own = lax.psum_scatter(partial, "hidden", scatter_dimension=1, tiled=True)
    features = own.reshape(examples, -1).astype(jnp.bfloat16)
    widened = features.astype(jnp.float32)
    every = lax.all_gather(features, "dp", axis=0, tiled=True).astype(jnp.float32)
    all_count = every.shape[0]
    weight = 1.0 / (jnp.sum(every * every, axis=0) / all_count + epsilon)
    partial_scores = jnp.dot(widened * weight, every.T, precision=HI)
    feat_total = features.shape[1] * lax.axis_size("hidden")
    scores = lax.psum_scatter(
        partial_scores / math.sqrt(feat_total), "hidden", scatter_dimension=1, tiled=True
    )
    return (features, scores)


def solution(mesh):
    placed = (
        P(("groups", "dp"), "hidden"),
        P(("groups", "dp"), "hidden"),
        P("hidden", None),
        P("hidden", None),
        P(),
    )
    return jax.shard_map(
        per_device,
        mesh=mesh,
        in_specs=placed,
        out_specs=(P(("groups", "dp"), "hidden"), P(("groups", "dp"), "hidden")),
        check_vma=False,
    )
```

profile of v0, /device:TPU:0, one launch (start us, length us, event | category | flops | bytes accessed | tf_op | source)
XLA Modules:
  0.0 102.2 jit_solution(1430355380435664496)
XLA Ops:
  7.2 0.0 copy-start
  7.2 0.0 copy-start.2
  7.2 0.0 all-reduce.3.cloned.1.call-start
  7.2 8.5 %fusion.3 = f32[3072,64]{0,1:T(8,128)S(1)} fusion(bf16[3072,2048]{1,0:T(8,128)(2,1)} %param.6, bf16[2048,64]{0,1:T(8,128)(2,1)} %param.7), kind=kOutput, calls=%fused_computation.9 | convolution fusion | flops 805306368 | bytes 13631488 | tf_op jit(solution)/shard_map/dot_general | solution.py:14
  15.8 0.0 copy-done.2
  15.8 0.0 copy-start.3
  15.8 0.6 fusion.4
  16.4 0.8 copy.16
  17.1 0.0 all-reduce.3.cloned.1.call-update
  17.2 0.0 reduce-scatter.3.cloned.1.call-start
  17.2 0.0 copy-done
  17.2 6.4 %fusion.5 = f32[3072,128]{1,0:T(8,128)S(1)} fusion(bf16[3072,2048]{1,0:T(8,128)(2,1)} %param.5, bf16[2048,128]{1,0:T(8,128)(2,1)S(1)} %copy-done), kind=kOutput, calls=%fused_computation.11 | convolution fusion | flops 1610612736 | bytes 14680064 | tf_op jit(solution)/shard_map/dot_general | solution.py:17
  23.7 33.3 %all-reduce.3.cloned.1.call-done = f32[6,512,32]{1,2,0:T(8,128)} async-done(((f32[6,512,32]{1,2,0:T(8,128)}), f32[6,512,32]{1,2,0:T(8,128)}) %all-reduce.3.cloned.1.call-update) | async-done | bytes 393232 | tf_op jit(solution)/shard_map/psum | solution.py:16
  57.0 2.6 %fusion.6 = f32[6,32,128]{2,1,0:T(8,128)} fusion(f32[6,512,32]{1,2,0:T(8,128)} %all-reduce.3.cloned.1.call-done, f32[6,512,128]{2,1,0:T(8,128)S(1)} %bitcast.23), kind=kOutput, calls=%fused_computation.12 | convolution fusion | flops 150994944 | bytes 2064384 | tf_op jit(solution)/shard_map/esa,esb->eab/dot_general | solution.py:20
  59.5 0.0 reduce-scatter.3.cloned.1.call-update
  59.6 0.0 copy-done.3
  59.6 0.6 dynamic-slice
  60.8 18.0 %reduce-scatter.3.cloned.1.call-done = f32[6,8,128]{2,1,0:T(8,128)} async-done(((f32[6,32,128]{2,1,0:T(8,128)}), f32[6,8,128]{2,1,0:T(8,128)}) %reduce-scatter.3.cloned.1.call-update) | async-done | bytes 24592 | tf_op jit(solution)/shard_map/reduce_scatter | solution.py:26
  78.9 0.7 convert_element_type.12
  79.6 5.2 %all-gather = bf16[4,6,1024]{2,1,0:T(8,128)(2,1)S(1)} all-gather(bf16[1,6,1024]{2,1,0:T(8,128)(2,1)S(1)} %reshape.19), channel_id=1, replica_groups=mesh['groups'=2,'dp'=4,'hidden'=4] {'dp'}, dimensions={0}, use_global_device_ids=true | all-gather | bytes 61440 | tf_op jit(solution)/shard_map/all_gather | solution.py:29
  84.9 0.7 convert_bitcast_fusion
  85.7 0.0 copy-start.1
  85.7 0.1 convolution_multiply_fusion
  85.8 8.9 %all-reduce = f32[6,24]{1,0:T(8,128)S(1)} all-reduce(f32[6,24]{1,0:T(8,128)S(1)} %convolution_multiply_fusion), channel_id=3, replica_groups=mesh['groups'=2,'dp'=4,'hidden'=4] {'hidden'}, use_global_device_ids=true, to_apply=%region_3.0.clone | all-reduce | flops 144 | bytes 1152
  94.7 0.7 constant_dynamic-slice_fusion
  95.4 0.0 copy-done.1
  (5 shorter events, 0.1 us)
Async XLA Ops:
  7.2 10.0 %copy-start = (bf16[2048,128]{1,0:T(8,128)(2,1)S(1)}, bf16[2048,128]{1,0:T(8,128)(2,1)}, u32[]{:S(2)}) copy-start(bf16[2048,128]{1,0:T(8,128)(2,1)} %param.8) | copy-start | bytes 1572868
  7.2 8.6 %copy-start.2 = (f32[64,32]{0,1:T(8,128)S(1)}, f32[64,32]{0,1:T(8,128)}, u32[]{:S(2)}) copy-start(f32[64,32]{0,1:T(8,128)} %param.9) | copy-start | bytes 24580
  7.2 49.8 %all-reduce.3.cloned.1.call-start = ((), (), s32[]{:S(2)}) async-start(), calls=%async_computation.1 | async-start | bytes 786432 | tf_op jit(solution)/shard_map/psum | solution.py:16
  15.8 43.8 %copy-start.3 = (u32[32]{0:T(128)S(1)}, u32[32]{0:T(128)}, u32[]{:S(2)}) copy-start(u32[32]{0:T(128)} %constant.14) | copy-start | bytes 388
  17.2 61.7 %reduce-scatter.3.cloned.1.call-start = ((), (), s32[]{:S(2)}) async-start(), calls=%async_computation.2 | async-start | bytes 122880 | tf_op jit(solution)/shard_map/reduce_scatter | solution.py:26
  85.7 9.7 %copy-start.1 = (bf16[1,6,8,128]{3,1,2,0:T(8,128)(2,1)}, bf16[1,6,8,128]{3,1,2,0:T(8,128)(2,1)S(1)}, u32[]{:S(2)}) copy-start(bf16[1,6,8,128]{3,1,2,0:T(8,128)(2,1)S(1)} %copy.17) | copy-start | bytes 36868
Sparse Core Ops, SparseCore 0:
  17.3 39.6 all-reduce.2
  59.7 19.1 reduce-scatter.2
where the time goes:
time: 103 us; the launch traced here: 102 us
  waiting for transfers between devices  51.4 us (50%)
  matrix products  18.2 us (18%)
  between operations  14.8 us (14%)
  blocking collectives  14.1 us (14%)
  local copies, waits for them, and re-layouts  2.12 us (2%)
  other arithmetic  1.51 us (1%)
    psum x1, waiting for transfers between devices, partial_features(): rank_full = lax.psum(rank_part, 'hidden')  33.3 us
    reduce_scatter x1, waiting for transfers between devices, per_device(): own = lax.psum_scatter(partial, 'hidden', scatter_dimension=1, tiled=True)  18 us
    unnamed x1, blocking collectives  8.87 us
    dot_general x1, matrix products, partial_features(): jnp.dot(cotangent, up_factor_matrix, preferred_element_type=jnp.float32)  8.54 us
    dot_general x1, matrix products, partial_features(): jnp.dot(activations, input_sketch, preferred_element_type=jnp.float32)  6.43 us
    all_gather x1, blocking collectives, per_device(): lax.all_gather(features, 'dp', axis=0, tiled=True).astype(jnp.float32)  5.24 us
    dot_general x1, matrix products, partial_features(): return jnp.einsum('esa,esb->eab', rank_rows, input_rows, precision=HI)  2.56 us
  transfers between devices with their start and end apart: 2, of which 2 were waited for; matrix products, arithmetic and copies ran while one was open for 7% of the time, Pallas kernels for 0%

commit v1 on v0

--- a/solution.py
+++ b/solution.py
@@ -13,7 +13,11 @@
     examples = activations.shape[0] // SEQ
     backward_pass = jnp.dot(cotangent, up_factor_matrix, preferred_element_type=jnp.float32)
     rank_part = jnp.dot(backward_pass, rank_sketch, precision=HI)
-    rank_full = lax.psum(rank_part, "hidden")
+    rank_full = rank_part
+    for hop in (1, 2):
+        rank_full = rank_full + lax.ppermute(
+            rank_full, "hidden", [(dev, dev ^ hop) for dev in range(4)]
+        )
     input_part = jnp.dot(activations, input_sketch, preferred_element_type=jnp.float32)
     rank_rows = rank_full.reshape(examples, SEQ, rank_full.shape[1])
     input_rows = input_part.reshape(examples, SEQ, input_part.shape[1])

time: 103 us -> 94.3 us (0.916)
  waiting for transfers between devices: 51.4 us -> 41.8 us
  starting transfers between devices: 0.08 us -> 5.97 us
  matrix products: 18.2 us -> 14.3 us
    psum x1 -> x0, waiting for transfers between devices: 33.3 us -> none  [partial_features(): rank_full = lax.psum(rank_part, 'hidden')]
    ppermute x0 -> x2, waiting for transfers between devices: none -> 22.5 us  [partial_features(): lax.ppermute(rank_full, 'hidden', [(dev, dev ^ hop) for dev in range(4)])]
    ppermute x0 -> x2, starting transfers between devices: none -> 5.94 us  [partial_features(): lax.ppermute(rank_full, 'hidden', [(dev, dev ^ hop) for dev in range(4)])]
    dot_general x1, matrix products: 6.43 us -> 3.43 us  [partial_features(): jnp.dot(activations, input_sketch, preferred_element_type=jnp.float32)]
    reduce_scatter x1, waiting for transfers between devices: 18 us -> 19.3 us  [per_device(): own = lax.psum_scatter(partial, 'hidden', scatter_dimension=1, tiled=True)]
  transfers between devices with their start and end apart: 2 -> 3, of which waited for: 2 -> 3; matrix products, arithmetic and copies ran while one was open for 7% -> 4% of each run, Pallas kernels for 0% -> 0%
where the time goes in v1:
time: 94.3 us; the launch traced here: 94 us
  waiting for transfers between devices  41.8 us (44%)
  between operations  14.8 us (16%)
  matrix products  14.3 us (15%)
  blocking collectives  14.2 us (15%)
  starting transfers between devices  5.97 us (6%)
  other arithmetic  1.59 us (2%)
  local copies, waits for them, and re-layouts  1.35 us (1%)
    ppermute x2, waiting for transfers between devices, partial_features(): lax.ppermute(rank_full, 'hidden', [(dev, dev ^ hop) for dev in range(4)])  22.5 us
    reduce_scatter x1, waiting for transfers between devices, per_device(): own = lax.psum_scatter(partial, 'hidden', scatter_dimension=1, tiled=True)  19.3 us
    unnamed x1, blocking collectives  8.93 us
    dot_general x1, matrix products, partial_features(): jnp.dot(cotangent, up_factor_matrix, preferred_element_type=jnp.float32)  8.64 us
    ppermute x2, starting transfers between devices, partial_features(): lax.ppermute(rank_full, 'hidden', [(dev, dev ^ hop) for dev in range(4)])  5.94 us
    all_gather x1, blocking collectives, per_device(): lax.all_gather(features, 'dp', axis=0, tiled=True).astype(jnp.float32)  5.24 us
    dot_general x1, matrix products, partial_features(): jnp.dot(activations, input_sketch, preferred_element_type=jnp.float32)  3.43 us
  transfers between devices with their start and end apart: 3, of which 3 were waited for; matrix products, arithmetic and copies ran while one was open for 4% of the time, Pallas kernels for 0%

profile of v1, /device:TPU:0, one launch (start us, length us, event | category | flops | bytes accessed | tf_op | source)
XLA Modules:
  0.0 94.0 jit_solution(14600837359801776262)
XLA Ops:
  7.2 0.0 copy-start
  7.2 0.0 copy-start.2
  7.2 0.0 reduce-scatter.3.cloned.1.call-start
  7.2 0.0 copy-start.3
  7.2 8.6 %fusion.6 = f32[3072,64]{0,1:T(8,128)S(1)} fusion(bf16[3072,2048]{1,0:T(8,128)(2,1)} %param.6, bf16[2048,64]{0,1:T(8,128)(2,1)} %param.7), kind=kOutput, calls=%fused_computation.11 | convolution fusion | flops 805306368 | bytes 13631488 | tf_op jit(solution)/shard_map/dot_general | solution.py:14
  15.9 0.0 copy-done.2
  15.9 0.0 copy-start.4
  15.9 0.6 fusion.7
  16.5 3.1 %collective-permute-start = (f32[3072,32]{0,1:T(8,128)S(1)}, f32[3072,32]{0,1:T(8,128)S(1)}, u32[]{:S(2)}, u32[]{:S(2)}) collective-permute-start(f32[3072,32]{0,1:T(8,128)S(1)} %fusion.7), channel_id=1, source_target_pairs={{0,1},{1,0},{2,3},{3,2},{4,5},{5,4},{6,7},{7,6},{8,9},{9,8},{10,11... | collective-permute-start | bytes 1179656 | tf_op jit(solution)/shard_map/ppermute | solution.py:18
  19.6 9.1 %collective-permute-done = f32[3072,32]{0,1:T(8,128)S(1)} collective-permute-done((f32[3072,32]{0,1:T(8,128)S(1)}, f32[3072,32]{0,1:T(8,128)S(1)}, u32[]{:S(2)}, u32[]{:S(2)}) %collective-permute-start) | collective-permute-done | bytes 393248 | tf_op jit(solution)/shard_map/ppermute | solution.py:18
  28.7 2.8 %collective-permute-start.1 = (f32[3072,32]{0,1:T(8,128)S(1)}, f32[3072,32]{0,1:T(8,128)S(1)}, u32[]{:S(2)}, u32[]{:S(2)}) collective-permute-start(f32[3072,32]{0,1:T(8,128)S(1)} %add.20), channel_id=1, source_target_pairs={{0,2},{1,3},{2,0},{3,1},{4,6},{5,7},{6,4},{7,5},{8,10},{9,11},{10,... | collective-permute-start | bytes 1179656 | tf_op jit(solution)/shard_map/ppermute | solution.py:18
  31.6 0.0 copy-done
  31.6 0.0 copy-done.3
  31.6 3.4 %fusion.8 = f32[3072,128]{1,0:T(8,128)S(1)} fusion(bf16[3072,2048]{1,0:T(8,128)(2,1)S(1)} %copy-done.3, bf16[2048,128]{1,0:T(8,128)(2,1)S(1)} %copy-done), kind=kOutput, calls=%fused_computation.13 | convolution fusion | flops 1610612736 | bytes 14680064 | tf_op jit(solution)/shard_map/dot_general | solution.py:21
  35.0 13.4 %collective-permute-done.1 = f32[3072,32]{0,1:T(8,128)S(1)} collective-permute-done((f32[3072,32]{0,1:T(8,128)S(1)}, f32[3072,32]{0,1:T(8,128)S(1)}, u32[]{:S(2)}, u32[]{:S(2)}) %collective-permute-start.1) | collective-permute-done | bytes 393248 | tf_op jit(solution)/shard_map/ppermute | solution.py:18
  48.5 1.6 %fusion = f32[6,32,128]{2,1,0:T(8,128)} fusion(f32[6,512,128]{2,1,0:T(8,128)S(1)} %bitcast.21, f32[4,6,8,512]{3,2,1,0:T(8,128)S(1)} %bitcast.22), kind=kOutput, calls=%fused_computation.1 | convolution fusion | flops 150994944 | bytes 2064384 | tf_op jit(solution)/shard_map/esa,esb->eab/dot_general | solution.py:24
  50.0 0.0 reduce-scatter.3.cloned.1.call-update
  50.0 0.0 copy-done.4
  50.1 0.6 dynamic-slice
  51.3 19.3 %reduce-scatter.3.cloned.1.call-done = f32[6,8,128]{2,1,0:T(8,128)} async-done(((f32[6,32,128]{2,1,0:T(8,128)}), f32[6,8,128]{2,1,0:T(8,128)}) %reduce-scatter.3.cloned.1.call-update) | async-done | bytes 24592 | tf_op jit(solution)/shard_map/reduce_scatter | solution.py:30
  70.6 0.7 convert_element_type.12
  71.3 5.2 %all-gather = bf16[4,6,1024]{2,1,0:T(8,128)(2,1)S(1)} all-gather(bf16[1,6,1024]{2,1,0:T(8,128)(2,1)S(1)} %reshape.19), channel_id=1, replica_groups=mesh['groups'=2,'dp'=4,'hidden'=4] {'dp'}, dimensions={0}, use_global_device_ids=true | all-gather | bytes 61440 | tf_op jit(solution)/shard_map/all_gather | solution.py:33
  76.7 0.7 convert_bitcast_fusion
  77.4 0.0 copy-start.1
  77.4 0.1 convolution_multiply_fusion
  77.5 8.9 %all-reduce = f32[6,24]{1,0:T(8,128)S(1)} all-reduce(f32[6,24]{1,0:T(8,128)S(1)} %convolution_multiply_fusion), channel_id=3, replica_groups=mesh['groups'=2,'dp'=4,'hidden'=4] {'hidden'}, use_global_device_ids=true, to_apply=%region_2.0.clone | all-reduce | flops 144 | bytes 1152
  86.5 0.7 constant_dynamic-slice_fusion
  87.1 0.0 copy-done.1
  (7 shorter events, 0.2 us)
Async XLA Ops:
  7.2 24.4 %copy-start = (bf16[2048,128]{1,0:T(8,128)(2,1)S(1)}, bf16[2048,128]{1,0:T(8,128)(2,1)}, u32[]{:S(2)}) copy-start(bf16[2048,128]{1,0:T(8,128)(2,1)} %param.8) | copy-start | bytes 1572868
  7.2 8.7 %copy-start.2 = (f32[64,32]{0,1:T(8,128)S(1)}, f32[64,32]{0,1:T(8,128)}, u32[]{:S(2)}) copy-start(f32[64,32]{0,1:T(8,128)} %param.9) | copy-start | bytes 24580
  7.2 63.4 %reduce-scatter.3.cloned.1.call-start = ((), (), s32[]{:S(2)}) async-start(), calls=%async_computation.1 | async-start | bytes 122880 | tf_op jit(solution)/shard_map/reduce_scatter | solution.py:30
  7.2 24.3 %copy-start.3 = (bf16[3072,2048]{1,0:T(8,128)(2,1)S(1)}, bf16[3072,2048]{1,0:T(8,128)(2,1)}, u32[]{:S(2)}) copy-start(bf16[3072,2048]{1,0:T(8,128)(2,1)} %param.5) | copy-start | bytes 37748740
  15.9 34.2 %copy-start.4 = (u32[32]{0:T(128)S(1)}, u32[32]{0:T(128)}, u32[]{:S(2)}) copy-start(u32[32]{0:T(128)} %constant.14) | copy-start | bytes 388
  16.5 12.2 %collective-permute-start = (f32[3072,32]{0,1:T(8,128)S(1)}, f32[3072,32]{0,1:T(8,128)S(1)}, u32[]{:S(2)}, u32[]{:S(2)}) collective-permute-start(f32[3072,32]{0,1:T(8,128)S(1)} %fusion.7), channel_id=1, source_target_pairs={{0,1},{1,0},{2,3},{3,2},{4,5},{5,4},{6,7},{7,6},{8,9},{9,8},{10,11... | collective-permute-start | bytes 1179656 | tf_op jit(solution)/shard_map/ppermute | solution.py:18
  28.7 19.7 %collective-permute-start.1 = (f32[3072,32]{0,1:T(8,128)S(1)}, f32[3072,32]{0,1:T(8,128)S(1)}, u32[]{:S(2)}, u32[]{:S(2)}) collective-permute-start(f32[3072,32]{0,1:T(8,128)S(1)} %add.20), channel_id=1, source_target_pairs={{0,2},{1,3},{2,0},{3,1},{4,6},{5,7},{6,4},{7,5},{8,10},{9,11},{10,... | collective-permute-start | bytes 1179656 | tf_op jit(solution)/shard_map/ppermute | solution.py:18
  77.4 9.7 %copy-start.1 = (bf16[1,6,8,128]{3,1,2,0:T(8,128)(2,1)}, bf16[1,6,8,128]{3,1,2,0:T(8,128)(2,1)S(1)}, u32[]{:S(2)}) copy-start(bf16[1,6,8,128]{3,1,2,0:T(8,128)(2,1)S(1)} %copy.19) | copy-start | bytes 36868
Sparse Core Ops, SparseCore 0:
  50.2 20.3 reduce-scatter.2
